TPU v7x, 512 devices: a whole 4x8x8 slice. The times are simulated.
512 devices in a mesh: dp: 16 (over x, y_hi, core), ctx: 32 (over z, y_lo).
Axes of the slice: x: 4, y: 8 (y_hi: 2, y_lo: 4; y = y_hi * 4 + y_lo), z: 8, core: 2. Of those that a mesh axis runs over, the one named last changes fastest.
Arguments:
- queries: bfloat16 [16, 4096, 512], P('dp', 'ctx'), may hold values from -6 to 6
- keys: bfloat16 [16, 4096, 512], P('dp', 'ctx'), may hold values from -6 to 6
- values: bfloat16 [16, 4096, 512], P('dp', 'ctx'), may hold values from -6 to 6
- grad_out: bfloat16 [16, 4096, 8192], P('dp', 'ctx'), may hold values from -6 to 6
- out_weight: bfloat16 [512, 8192], P(None, 'ctx'), may hold values from -0.25 to 0.25
- residues: float32 [512, 16], P('ctx'), may hold values from -0.125 to 0.125
- decays: float32 [512, 16], P('ctx'), may hold values from 1.2207031e-05 to 0.1
Outputs:
- grad_queries: bfloat16 [16, 4096, 512], P('dp', None, 'ctx')
- grad_keys: bfloat16 [16, 4096, 512], P('dp', None, 'ctx')
- grad_values: bfloat16 [16, 4096, 512], P('dp', None, 'ctx')
- grad_weight: float32 [512, 8192], P(None, 'ctx')
- grad_residues: float32 [512, 16], P('ctx')
- grad_decays: float32 [512, 16], P('ctx')
All inputs are finite; a program needn't handle non-finite values.
Results may differ from a plain program's by a relative error of at most 0.017.
Values may be sent and summed in bfloat16 or wider, within the bound.
No kernel may reach another device: no remote copies, remote signals or barrier semaphores. Data moves between devices by JAX's collectives and lax.ppermute only.
A program may use at most 128 MiB of HBM per device.

v0:
```python
import math
import jax
import jax.numpy as jnp
from jax import lax
from jax.sharding import PartitionSpec as P

FFT_COLS = 128
HIGHEST = lax.Precision.HIGHEST


def fourier_tables(fft_rows, fft_cols):
    total = fft_rows * fft_cols
    row_index = jnp.arange(fft_rows, dtype=jnp.int32)
    col_index = jnp.arange(fft_cols, dtype=jnp.int32)
    first = (row_index[:, None] * row_index[None, :] % fft_rows).astype(jnp.float32) * (
        2.0 * math.pi / fft_rows
    )
    twist = (row_index[:, None] * col_index[None, :] % total).astype(jnp.float32) * (
        2.0 * math.pi / total
    )
    second = (col_index[:, None] * col_index[None, :] % fft_cols).astype(jnp.float32) * (
        2.0 * math.pi / fft_cols
    )
    return (
        (jnp.cos(first), -jnp.sin(first)),
        (jnp.cos(twist), -jnp.sin(twist)),
        (jnp.cos(second), -jnp.sin(second)),
    )


def complex_product(left_re, left_im, right_re, right_im):
    return (left_re * right_re - left_im * right_im, left_re * right_im + left_im * right_re)


def apply_middle(table_re, table_im, data_re):

    def single(table, data):
        return jnp.einsum("kn,cnm->ckm", table, data, precision=HIGHEST)

    return (single(table_re, data_re), single(table_im, data_re))


def apply_last(table_re, table_im, data_re, data_im):

    def single(data, table):
        return jnp.einsum("ckm,mj->ckj", data, table, precision=HIGHEST)

    return (
        single(data_re, table_re) - single(data_im, table_im),
        single(data_im, table_re) + single(data_re, table_im),
    )


def forward_transform(signal, tables):
    (first_re, first_im), (twist_re, twist_im), (second_re, second_im) = tables
    section_re, section_im = apply_middle(first_re, first_im, signal)
    section_re, section_im = complex_product(section_re, section_im, twist_re, twist_im)
    return apply_last(second_re, second_im, section_re, section_im)


def inverse_transform(spec_re, spec_im, tables):
    (first_re, first_im), (twist_re, twist_im), (second_re, second_im) = tables
    section_re, section_im = apply_last(second_re, -second_im, spec_re, spec_im)
    section_re, section_im = complex_product(section_re, section_im, twist_re, -twist_im)
    result = jnp.einsum("kn,cnm->ckm", first_re, section_re, precision=HIGHEST) + jnp.einsum(
        "kn,cnm->ckm", first_im, section_im, precision=HIGHEST
    )
    total = first_re.shape[0] * second_re.shape[0]
    return result / float(total)


def padded_grid(signal, fft_rows, fft_cols):
    channels, seq_len = signal.shape
    padded = jnp.concatenate(
        [signal, jnp.zeros((channels, fft_rows * fft_cols - seq_len), jnp.float32)], axis=1
    )
    return padded.reshape(channels, fft_rows, fft_cols)


def leading_part(grid, seq_len):
    return grid.reshape(grid.shape[0], -1)[:, :seq_len]


def channels_first(block):
    return block[0].astype(jnp.float32).T


def rounded_sum(terms):
    rounded = lax.optimization_barrier(terms.astype(jnp.bfloat16))
    return jnp.sum(rounded.astype(jnp.float32), axis=0)


def axis_pairs(size, mask):
    return [(index, index ^ mask) for index in range(size)]


def ctx_masks(size):
    bits = [1 << b for b in range(size.bit_length() - 1)]
    low = [m for m in bits if m < 4]
    high = [m for m in bits if m >= 4]
    return tuple(reversed(high[1:])) + tuple(reversed(low[1:])) + tuple(high[:1]) + tuple(low[:1])


def doubling_gather(block, axis, masks):
    size = lax.axis_size(axis)
    held = block
    for mask in masks:
        held = jnp.concatenate([held, lax.ppermute(held, axis, axis_pairs(size, mask))], axis=0)
    return held


def unpermute_blocks(rows, axis, masks):
    size = lax.axis_size(axis)
    me = lax.axis_index(axis)
    wanted = me ^ jnp.arange(size, dtype=jnp.int32)
    place = jnp.zeros_like(wanted)
    for step, mask in enumerate(masks):
        place = place | (wanted & mask != 0).astype(jnp.int32) << step
    blocks = rows.reshape(size, rows.shape[0] // size, rows.shape[1])
    return jnp.take(blocks, place, axis=0).reshape(rows.shape)


def dp_masks(size):
    bits = [1 << b for b in range(size.bit_length() - 1)]
    return tuple(bits[:1]) + tuple(bits[2:]) + tuple(bits[1:2])


def summed_over_dp(grad_weight, grad_residues, grad_decays):
    size = lax.axis_size("dp")
    width = grad_weight.shape[1]
    extra = jnp.stack([grad_residues.reshape(-1), grad_decays.reshape(-1)])
    extra = jnp.pad(extra, ((0, 0), (0, width - extra.shape[1])))
    rows = grad_weight.shape[0] + 2
    padded_rows = -(-rows // size) * size
    held = jnp.concatenate(
        [grad_weight, extra, jnp.zeros((padded_rows - rows, width), jnp.float32)], axis=0
    )
    me = lax.axis_index("dp")
    masks = dp_masks(size)
    for mask in masks:
        half = held.shape[0] // 2
        low, high = (held[:half], held[half:])
        upper = me & mask != 0
        keep = jnp.where(upper, high, low)
        send = jnp.where(upper, low, high)
        held = keep + lax.ppermute(send, "dp", axis_pairs(size, mask))
    for mask in reversed(masks):
        other = lax.ppermute(held, "dp", axis_pairs(size, mask))
        upper = me & mask != 0
        held = jnp.where(upper, jnp.concatenate([other, held]), jnp.concatenate([held, other]))
    count = grad_residues.size
    weight = held[: grad_weight.shape[0]]
    residue_sum = held[grad_weight.shape[0], :count].reshape(grad_residues.shape)
    decay_sum = held[grad_weight.shape[0] + 1, :count].reshape(grad_decays.shape)
    return (weight, residue_sum, decay_sum)


def body(queries, keys, values, grad_out, out_weight, residues, decays):
    channels = out_weight.shape[0]
    block_width = out_weight.shape[1]
    tok_rows = grad_out.shape[1]
    grad_cols = lax.all_to_all(grad_out, "ctx", split_axis=2, concat_axis=1, tiled=True)
    shard_piece = lax.all_gather(out_weight, "ctx", axis=1, tiled=True)
    blocks = shard_piece.shape[1] // block_width
    partial_value = grad_out[0]
    partial_value = partial_value.reshape(tok_rows, blocks, block_width)
    weight_part = shard_piece.reshape(channels, blocks, block_width)
    terms = jnp.einsum(
        "tks,cks->ktc", partial_value, weight_part, preferred_element_type=jnp.float32
    )
    gated_sum = rounded_sum(terms)
    grad_gated = gated_sum.astype(jnp.bfloat16)[None]
    query_ch, key_ch, value_ch, gated_grad_ch = (
        lax.all_to_all(queries, "ctx", split_axis=2, concat_axis=1, tiled=True),
        lax.all_to_all(keys, "ctx", split_axis=2, concat_axis=1, tiled=True),
        lax.all_to_all(values, "ctx", split_axis=2, concat_axis=1, tiled=True),
        lax.all_to_all(grad_gated, "ctx", split_axis=2, concat_axis=1, tiled=True),
    )
    grad_gated_full = channels_first(gated_grad_ch)
    seq_len = query_ch.shape[1]
    fft_rows = 2 * seq_len // FFT_COLS
    tables = fourier_tables(fft_rows, FFT_COLS)
    query_full = channels_first(query_ch)
    key_full = channels_first(key_ch)
    value_full = channels_first(value_ch)
    positions = jnp.arange(seq_len).astype(jnp.float32)
    decay_terms = jnp.exp(-decays[:, :, None] * positions[None, None, :])
    filter_taps = jnp.sum(residues[:, :, None] * decay_terms, axis=1)
    product = key_full * value_full
    grad_conv = grad_gated_full * query_full
    prod_re, prod_im = forward_transform(padded_grid(product, fft_rows, FFT_COLS), tables)
    taps_re, taps_im = forward_transform(padded_grid(filter_taps, fft_rows, FFT_COLS), tables)
    grad_re, grad_im = forward_transform(padded_grid(grad_conv, fft_rows, FFT_COLS), tables)
    conv_out = leading_part(
        inverse_transform(*complex_product(prod_re, prod_im, taps_re, taps_im), tables), seq_len
    )
    grad_product = leading_part(
        inverse_transform(*complex_product(taps_re, -taps_im, grad_re, grad_im), tables), seq_len
    )
    grad_taps = leading_part(
        inverse_transform(*complex_product(prod_re, -prod_im, grad_re, grad_im), tables), seq_len
    )
    gated_t = (query_full * conv_out).astype(jnp.bfloat16)
    grad_queries = (grad_gated_full * conv_out).T.astype(jnp.bfloat16)[None]
    grad_keys = (grad_product * value_full).T.astype(jnp.bfloat16)[None]
    grad_values = (grad_product * key_full).T.astype(jnp.bfloat16)[None]
    ctx_size = lax.axis_size("ctx")
    gather_masks = ctx_masks(ctx_size)
    gathered = doubling_gather(gated_t, "ctx", gather_masks)
    partial_value = lax.dot_general(
        gathered, grad_cols[0], (((1,), (0,)), ((), ())), preferred_element_type=jnp.float32
    )
    grad_weight = unpermute_blocks(partial_value, "ctx", gather_masks)
    grad_residues = jnp.sum(grad_taps[:, None, :] * decay_terms, axis=2)
    grad_decays = -residues * jnp.sum(
        (grad_taps * positions[None, :])[:, None, :] * decay_terms, axis=2
    )
    grad_weight, grad_residues, grad_decays = summed_over_dp(
        grad_weight, grad_residues, grad_decays
    )
    return (grad_queries, grad_keys, grad_values, grad_weight, grad_residues, grad_decays)


def solution(mesh):
    placed = (
        P("dp", "ctx", None),
        P("dp", "ctx", None),
        P("dp", "ctx", None),
        P("dp", "ctx", None),
        P(None, "ctx"),
        P("ctx", None),
        P("ctx", None),
    )
    return jax.shard_map(
        body,
        mesh=mesh,
        in_specs=placed,
        out_specs=(
            P("dp", None, "ctx"),
            P("dp", None, "ctx"),
            P("dp", None, "ctx"),
            P(None, "ctx"),
            P("ctx", None),
            P("ctx", None),
        ),
        check_vma=False,
    )
```

profile of v0, /device:TPU:107, one launch (start us, length us, event | category | flops | bytes accessed | tf_op | source)
XLA Modules:
  0.0 560.3 jit_solution(7011197182111758625)
XLA Ops:
  7.2 1.8 copy.70
  12.7 10.7 %all-to-all-start.3 = ((bf16[32,2,1024]{2,1,0:T(2,128)(2,1)}), bf16[32,2,1024]{2,1,0:T(2,128)(2,1)S(1)}, u32[]{:S(2)}, u32[]{:S(2)}) async-start(bf16[32,2,1024]{2,1,0:T(2,128)(2,1)} %reshape.256), calls=%async_computation.3 | async-start | bytes 262144 | tf_op jit(solution)/shard_map/all_to_all | solution.py:174
  26.6 4.8 all-to-all-done.3
  31.4 5.9 %all-to-all-start.1 = ((bf16[32,2,1024]{2,1,0:T(2,128)(2,1)}), bf16[32,2,1024]{2,1,0:T(2,128)(2,1)S(1)}, u32[]{:S(2)}, u32[]{:S(2)}) async-start(bf16[32,2,1024]{2,1,0:T(2,128)(2,1)} %reshape.254), calls=%async_computation.1 | async-start | bytes 262144 | tf_op jit(solution)/shard_map/all_to_all | solution.py:175
  41.2 2.2 copy.89
  43.8 3.4 all-to-all-done.1
  47.2 7.3 %all-to-all-start.2 = ((bf16[32,2,1024]{2,1,0:T(2,128)(2,1)}), bf16[32,2,1024]{2,1,0:T(2,128)(2,1)S(1)}, u32[]{:S(2)}, u32[]{:S(2)}) async-start(bf16[32,2,1024]{2,1,0:T(2,128)(2,1)} %reshape.252), calls=%async_computation.2 | async-start | bytes 262144 | tf_op jit(solution)/shard_map/all_to_all | solution.py:176
  54.9 9.4 %all-to-all-done.2 = bf16[32,2,1024]{2,1,0:T(2,128)(2,1)S(1)} async-done(((bf16[32,2,1024]{2,1,0:T(2,128)(2,1)}), bf16[32,2,1024]{2,1,0:T(2,128)(2,1)S(1)}, u32[]{:S(2)}, u32[]{:S(2)}) %all-to-all-start.2) | async-done | bytes 131104 | tf_op jit(solution)/shard_map/all_to_all | solution.py:176
  70.8 139.5 %all-gather.2.cloned.1.call-done = bf16[512,8192]{0,1:T(8,128)(2,1)} async-done(((bf16[512,256]{0,1:T(8,128)(2,1)}), bf16[512,8192]{0,1:T(8,128)(2,1)}) %all-gather.2.cloned.1.call-update) | async-done | bytes 8388624 | tf_op jit(solution)/shard_map/all_gather | solution.py:163
  210.3 8.2 %convolution_convert_fusion = bf16[32,128,512]{2,1,0:T(8,128)(2,1)} fusion(bf16[512,32,256]{0,2,1:T(8,128)(2,1)} %bitcast.286, bf16[128,32,256]{2,1,0:T(8,128)(2,1)S(1)} %bitcast.287), kind=kOutput, calls=%fused_computation.5 | convolution fusion | flops 1075838976 | bytes 14680064 | tf_op jit(solution)/shard_map/tks,cks->ktc/dot_general | solution.py:168
  218.5 2.9 reduce_sum.39
  223.6 9.0 %all-to-all-start = ((bf16[32,2,1024]{2,1,0:T(2,128)(2,1)}), bf16[32,2,1024]{2,1,0:T(2,128)(2,1)S(1)}, u32[]{:S(2)}, u32[]{:S(2)}) async-start(bf16[32,2,1024]{2,1,0:T(2,128)(2,1)} %reshape.258), calls=%async_computation | async-start | bytes 262144 | tf_op jit(solution)/shard_map/all_to_all | solution.py:177
  233.5 6.9 %all-to-all-done = bf16[32,2,1024]{2,1,0:T(2,128)(2,1)S(1)} async-done(((bf16[32,2,1024]{2,1,0:T(2,128)(2,1)}), bf16[32,2,1024]{2,1,0:T(2,128)(2,1)S(1)}, u32[]{:S(2)}, u32[]{:S(2)}) %all-to-all-start) | async-done | bytes 131104 | tf_op jit(solution)/shard_map/all_to_all | solution.py:177
  251.3 2.5 multiply_reduce_fusion.1
  265.0 3.1 collective-permute-start
  268.2 7.2 %collective-permute-done = bf16[16,4096]{1,0:T(8,128)(2,1)S(1)} collective-permute-done((bf16[16,4096]{1,0:T(8,128)(2,1)S(1)}, bf16[16,4096]{1,0:T(8,128)(2,1)S(1)}, u32[]{:S(2)}, u32[]{:S(2)}) %collective-permute-start) | collective-permute-done | bytes 131104 | tf_op jit(solution)/shard_map/ppermute | solution.py:108
  275.5 3.6 collective-permute-start.1
  279.0 10.0 %collective-permute-done.1 = bf16[32,4096]{1,0:T(8,128)(2,1)S(1)} collective-permute-done((bf16[32,4096]{1,0:T(8,128)(2,1)S(1)}, bf16[32,4096]{1,0:T(8,128)(2,1)S(1)}, u32[]{:S(2)}, u32[]{:S(2)}) %collective-permute-start.1) | collective-permute-done | bytes 262176 | tf_op jit(solution)/shard_map/ppermute | solution.py:108
  290.5 2.0 collective-permute-start.2
  292.6 7.1 %copy.85 = bf16[1,128,8192]{1,0,2:T(2,128)(2,1)} copy(bf16[1,128,8192]{2,1,0:T(8,128)(2,1)S(1)} %copy-done) | data formatting | bytes 4194304 | tf_op args[3]
  299.6 45.2 %reduce.13 = bf16[8192,128]{1,0:T(8,128)(2,1)S(1)} reduce(bf16[8192,1,128]{2,1,0:T(2,128)(2,1)} %bitcast.288, bf16[]{:T(256)} %broadcast.471), dimensions={1}, to_apply=%bitcast.254.reduce_sub_computation | reduce | bytes 4194306
  344.8 2.1 reshape.260
  346.9 8.6 %all-to-all-start.4 = ((bf16[32,2,16384]{2,1,0:T(2,128)(2,1)}), bf16[32,2,16384]{2,1,0:T(2,128)(2,1)S(1)}, u32[]{:S(2)}, u32[]{:S(2)}) async-start(bf16[32,2,16384]{2,1,0:T(2,128)(2,1)} %reshape.260), calls=%async_computation.4 | async-start | bytes 4194304 | tf_op jit(solution)/shard_map/all_to_all | solution.py:162
  356.7 2.2 collective-permute-start.3
  361.2 1.9 constant_dynamic-update-slice_fusion.1
  363.2 67.6 %collective-permute-done.3 = bf16[128,4096]{1,0:T(8,128)(2,1)S(1)} collective-permute-done((bf16[128,4096]{1,0:T(8,128)(2,1)S(1)}, bf16[128,4096]{1,0:T(8,128)(2,1)S(1)}, u32[]{:S(2)}, u32[]{:S(2)}) %collective-permute-start.3) | collective-permute-done | bytes 1048608 | tf_op jit(solution)/shard_map/ppermute | solution.py:108
  431.9 1.9 copy-done.16
  433.9 1.9 collective-permute-start.4
  436.1 6.8 %reshape.261 = bf16[8192,1,128]{2,1,0:T(2,128)(2,1)} reshape(bf16[32,2,16384]{2,1,0:T(2,128)(2,1)S(1)} %all-to-all-done.4) | data formatting | bytes 4194304
  442.9 2.5 copy.88
  445.4 2.9 copy.86
  448.5 32.8 %collective-permute-done.4 = bf16[256,4096]{1,0:T(8,128)(2,1)} collective-permute-done((bf16[256,4096]{1,0:T(8,128)(2,1)}, bf16[256,4096]{1,0:T(8,128)(2,1)}, u32[]{:S(2)}, u32[]{:S(2)}) %collective-permute-start.4) | collective-permute-done | bytes 2097184 | tf_op jit(solution)/shard_map/ppermute | solution.py:108
  481.3 3.1 constant_dynamic-update-slice_fusion.5
  484.4 4.2 fusion.323
  490.6 4.7 collective-permute-start.5
  496.6 1.9 collective-permute-start.6
  499.3 4.0 collective-permute-done.6
  503.4 2.4 collective-permute-start.7
  506.6 3.5 collective-permute-done.7
  510.2 2.3 collective-permute-start.8
  513.3 5.7 %collective-permute-done.8 = f32[33,256]{1,0:T(8,128)S(1)} collective-permute-done((f32[33,256]{1,0:T(8,128)S(1)}, f32[33,256]{1,0:T(8,128)S(1)}, u32[]{:S(2)}, u32[]{:S(2)}) %collective-permute-start.8) | collective-permute-done | bytes 33824 | tf_op jit(solution)/shard_map/ppermute | solution.py:146
  519.0 1.9 collective-permute-start.9
  521.7 5.9 %collective-permute-done.9 = f32[33,256]{1,0:T(8,128)S(1)} collective-permute-done((f32[33,256]{1,0:T(8,128)S(1)}, f32[33,256]{1,0:T(8,128)S(1)}, u32[]{:S(2)}, u32[]{:S(2)}) %collective-permute-start.9) | collective-permute-done | bytes 33824 | tf_op jit(solution)/shard_map/ppermute | solution.py:148
  527.7 2.3 collective-permute-start.10
  531.0 3.2 collective-permute-done.10
  534.3 2.6 collective-permute-start.11
  538.0 2.4 collective-permute-done.11
  540.4 9.4 %collective-permute-start.12 = (f32[264,256]{1,0:T(8,128)S(1)}, f32[264,256]{1,0:T(8,128)S(1)}, u32[]{:S(2)}, u32[]{:S(2)}) collective-permute-start(f32[264,256]{1,0:T(8,128)S(1)} %maximum_select_fusion.1), channel_id=1, source_target_pairs={{0,32},{32,0},{64,96},{96,64},{128,160},{160,128},{192,224},{224,1... | collective-permute-start | bytes 811016 | tf_op jit(solution)/shard_map/ppermute | solution.py:148
  (158 shorter events, 61.6 us)
Async XLA Ops:
  7.2 203.1 %all-gather.2.cloned.1.call-start = ((), (), s32[]{:S(2)}) async-start(), calls=%async_computation.5 | async-start | bytes 8650752 | tf_op jit(solution)/shard_map/all_gather | solution.py:163
  12.7 18.6 %all-to-all-start.3 = ((bf16[32,2,1024]{2,1,0:T(2,128)(2,1)}), bf16[32,2,1024]{2,1,0:T(2,128)(2,1)S(1)}, u32[]{:S(2)}, u32[]{:S(2)}) async-start(bf16[32,2,1024]{2,1,0:T(2,128)(2,1)} %reshape.256), calls=%async_computation.3 | async-start | bytes 262144 | tf_op jit(solution)/shard_map/all_to_all | solution.py:174
  31.4 15.8 %all-to-all-start.1 = ((bf16[32,2,1024]{2,1,0:T(2,128)(2,1)}), bf16[32,2,1024]{2,1,0:T(2,128)(2,1)S(1)}, u32[]{:S(2)}, u32[]{:S(2)}) async-start(bf16[32,2,1024]{2,1,0:T(2,128)(2,1)} %reshape.254), calls=%async_computation.1 | async-start | bytes 262144 | tf_op jit(solution)/shard_map/all_to_all | solution.py:175
  47.2 17.1 %all-to-all-start.2 = ((bf16[32,2,1024]{2,1,0:T(2,128)(2,1)}), bf16[32,2,1024]{2,1,0:T(2,128)(2,1)S(1)}, u32[]{:S(2)}, u32[]{:S(2)}) async-start(bf16[32,2,1024]{2,1,0:T(2,128)(2,1)} %reshape.252), calls=%async_computation.2 | async-start | bytes 262144 | tf_op jit(solution)/shard_map/all_to_all | solution.py:176
  54.6 186.1 %copy-start.2 = (f32[1,32,128,16]{2,1,3,0:T(8,128)}, f32[1,32,128,16]{2,1,3,0:T(8,128)S(1)}, u32[]{:S(2)}) copy-start(f32[1,32,128,16]{2,1,3,0:T(8,128)S(1)} %copy.84) | copy-start | bytes 786436
  54.9 10.2 %copy-start.6 = (f32[1,32,128,16]{2,1,3,0:T(8,128)}, f32[1,32,128,16]{2,1,3,0:T(8,128)S(1)}, u32[]{:S(2)}) copy-start(f32[1,32,128,16]{2,1,3,0:T(8,128)S(1)} %copy.78) | copy-start | bytes 786436
  64.6 0.7 copy-start.8
  218.5 14.1 %copy-start.14 = (f32[16,64,128]{2,1,0:T(8,128)S(1)}, f32[16,64,128]{2,1,0:T(8,128)}, u32[]{:S(2)}) copy-start(f32[16,64,128]{2,1,0:T(8,128)} %fusion.48) | copy-start | bytes 1572868
  223.6 16.8 %all-to-all-start = ((bf16[32,2,1024]{2,1,0:T(2,128)(2,1)}), bf16[32,2,1024]{2,1,0:T(2,128)(2,1)S(1)}, u32[]{:S(2)}, u32[]{:S(2)}) async-start(bf16[32,2,1024]{2,1,0:T(2,128)(2,1)} %reshape.258), calls=%async_computation | async-start | bytes 262144 | tf_op jit(solution)/shard_map/all_to_all | solution.py:177
  240.7 4.5 copy-start.4
  241.0 4.1 copy-start.1
  247.7 3.6 copy-start.15
  260.6 3.6 copy-start.3
  261.4 31.1 %copy-start = (bf16[1,128,8192]{2,1,0:T(8,128)(2,1)S(1)}, bf16[1,128,8192]{2,1,0:T(8,128)(2,1)}, u32[]{:S(2)}) copy-start(bf16[1,128,8192]{2,1,0:T(8,128)(2,1)} %param.10) | copy-start | bytes 6291460
  264.2 11.3 %copy-start.11 = (f32[2,8,64,128]{3,1,2,0:T(8,128)}, f32[2,8,64,128]{3,1,2,0:T(8,128)S(1)}, u32[]{:S(2)}) copy-start(f32[2,8,64,128]{3,1,2,0:T(8,128)S(1)} %copy.122) | copy-start | bytes 1572868
  265.0 10.4 %collective-permute-start = (bf16[16,4096]{1,0:T(8,128)(2,1)S(1)}, bf16[16,4096]{1,0:T(8,128)(2,1)S(1)}, u32[]{:S(2)}, u32[]{:S(2)}) collective-permute-start(bf16[16,4096]{1,0:T(8,128)(2,1)S(1)} %get-tuple-element.12), channel_id=1, source_target_pairs={{0,16},{1,17},{2,18},{3,19},{4,20},{5,21},{6,22},{7,23},{8,24},{9,... | collective-permute-start | bytes 393224 | tf_op jit(solution)/shard_map/ppermute | solution.py:108
  275.5 13.5 %collective-permute-start.1 = (bf16[32,4096]{1,0:T(8,128)(2,1)S(1)}, bf16[32,4096]{1,0:T(8,128)(2,1)S(1)}, u32[]{:S(2)}, u32[]{:S(2)}) collective-permute-start(bf16[32,4096]{1,0:T(8,128)(2,1)S(1)} %pad_maximum_fusion.4), channel_id=1, source_target_pairs={{0,8},{1,9},{2,10},{3,11},{4,12},{5,13},{6,14},{7,15},{8,0},{9,1},... | collective-permute-start | bytes 786440 | tf_op jit(solution)/shard_map/ppermute | solution.py:108
  289.0 0.7 copy-start.10
  290.5 64.9 %collective-permute-start.2 = (bf16[64,4096]{1,0:T(8,128)(2,1)}, bf16[64,4096]{1,0:T(8,128)(2,1)}, u32[]{:S(2)}, u32[]{:S(2)}) collective-permute-start(bf16[64,4096]{1,0:T(8,128)(2,1)} %pad_maximum_fusion.1), channel_id=1, source_target_pairs={{0,2},{1,3},{2,0},{3,1},{4,6},{5,7},{6,4},{7,5},{8,10},{9,11},{10,... | collective-permute-start | bytes 1572872 | tf_op jit(solution)/shard_map/ppermute | solution.py:108
  346.9 89.2 %all-to-all-start.4 = ((bf16[32,2,16384]{2,1,0:T(2,128)(2,1)}), bf16[32,2,16384]{2,1,0:T(2,128)(2,1)S(1)}, u32[]{:S(2)}, u32[]{:S(2)}) async-start(bf16[32,2,16384]{2,1,0:T(2,128)(2,1)} %reshape.260), calls=%async_computation.4 | async-start | bytes 4194304 | tf_op jit(solution)/shard_map/all_to_all | solution.py:162
  356.7 74.1 %collective-permute-start.3 = (bf16[128,4096]{1,0:T(8,128)(2,1)S(1)}, bf16[128,4096]{1,0:T(8,128)(2,1)S(1)}, u32[]{:S(2)}, u32[]{:S(2)}) collective-permute-start(bf16[128,4096]{1,0:T(8,128)(2,1)S(1)} %pad_maximum_fusion), channel_id=1, source_target_pairs={{0,4},{1,5},{2,6},{3,7},{4,0},{5,1},{6,2},{7,3},{8,12},{9,13},{10,... | collective-permute-start | bytes 3145736 | tf_op jit(solution)/shard_map/ppermute | solution.py:108
  431.9 1.9 copy-start.16
  433.9 47.5 %collective-permute-start.4 = (bf16[256,4096]{1,0:T(8,128)(2,1)}, bf16[256,4096]{1,0:T(8,128)(2,1)}, u32[]{:S(2)}, u32[]{:S(2)}) collective-permute-start(bf16[256,4096]{1,0:T(8,128)(2,1)} %get-tuple-element.19), channel_id=1, source_target_pairs={{0,1},{1,0},{2,3},{3,2},{4,5},{5,4},{6,7},{7,6},{8,9},{9,8},{10,11... | collective-permute-start | bytes 6291464 | tf_op jit(solution)/shard_map/ppermute | solution.py:108
  448.3 36.1 %copy-start.13 = (bf16[1,32,128,256]{3,2,1,0:T(8,128)(2,1)S(1)}, bf16[1,32,128,256]{3,2,1,0:T(8,128)(2,1)}, u32[]{:S(2)}) copy-start(bf16[1,32,128,256]{3,2,1,0:T(8,128)(2,1)} %copy.86) | copy-start | bytes 6291460
  490.6 5.9 %collective-permute-start.5 = (f32[264,256]{1,0:T(8,128)S(1)}, f32[264,256]{1,0:T(8,128)S(1)}, u32[]{:S(2)}, u32[]{:S(2)}) collective-permute-start(f32[264,256]{1,0:T(8,128)S(1)} %slice_select_fusion), channel_id=1, source_target_pairs={{0,32},{32,0},{64,96},{96,64},{128,160},{160,128},{192,224},{224,1... | collective-permute-start | bytes 811016 | tf_op jit(solution)/shard_map/ppermute | solution.py:146
  496.6 6.8 %collective-permute-start.6 = (f32[132,256]{1,0:T(8,128)S(1)}, f32[132,256]{1,0:T(8,128)S(1)}, u32[]{:S(2)}, u32[]{:S(2)}) collective-permute-start(f32[132,256]{1,0:T(8,128)S(1)} %slice_select_fusion.1), channel_id=1, source_target_pairs={{0,128},{32,160},{64,192},{96,224},{128,0},{160,32},{192,64},{224,... | collective-permute-start | bytes 405512 | tf_op jit(solution)/shard_map/ppermute | solution.py:146
  503.4 33.6 %copy-start.7 = (f32[1,32,128,16]{2,1,3,0:T(8,128)S(1)}, f32[1,32,128,16]{2,1,3,0:T(8,128)}, u32[]{:S(2)}) copy-start(f32[1,32,128,16]{2,1,3,0:T(8,128)} %copy-done.6) | copy-start | bytes 786436
  503.4 33.6 %copy-start.9 = (f32[1,32,128,16]{2,1,3,0:T(8,128)S(1)}, f32[1,32,128,16]{2,1,3,0:T(8,128)}, u32[]{:S(2)}) copy-start(f32[1,32,128,16]{2,1,3,0:T(8,128)} %copy-done.8) | copy-start | bytes 786436
  503.4 6.7 %collective-permute-start.7 = (f32[66,256]{1,0:T(8,128)S(1)}, f32[66,256]{1,0:T(8,128)S(1)}, u32[]{:S(2)}, u32[]{:S(2)}) collective-permute-start(f32[66,256]{1,0:T(8,128)S(1)} %slice_select_fusion.2), channel_id=1, source_target_pairs={{0,256},{32,288},{64,320},{96,352},{128,384},{160,416},{192,448},{... | collective-permute-start | bytes 202760 | tf_op jit(solution)/shard_map/ppermute | solution.py:146
  510.2 39.6 %copy-start.5 = (f32[1,32,128,16]{2,1,3,0:T(8,128)S(1)}, f32[1,32,128,16]{2,1,3,0:T(8,128)}, u32[]{:S(2)}) copy-start(f32[1,32,128,16]{2,1,3,0:T(8,128)} %copy-done.4) | copy-start | bytes 786436
  510.2 39.6 %copy-start.12 = (f32[2,8,64,128]{3,1,2,0:T(8,128)S(1)}, f32[2,8,64,128]{3,1,2,0:T(8,128)}, u32[]{:S(2)}) copy-start(f32[2,8,64,128]{3,1,2,0:T(8,128)} %copy-done.11) | copy-start | bytes 1572868
  510.2 8.8 %collective-permute-start.8 = (f32[33,256]{1,0:T(8,128)S(1)}, f32[33,256]{1,0:T(8,128)S(1)}, u32[]{:S(2)}, u32[]{:S(2)}) collective-permute-start(f32[33,256]{1,0:T(8,128)S(1)} %slice_select_fusion.3), channel_id=1, source_target_pairs={{0,64},{32,96},{64,0},{96,32},{128,192},{160,224},{192,128},{224,1... | collective-permute-start | bytes 101384 | tf_op jit(solution)/shard_map/ppermute | solution.py:146
  519.0 8.7 %collective-permute-start.9 = (f32[33,256]{1,0:T(8,128)S(1)}, f32[33,256]{1,0:T(8,128)S(1)}, u32[]{:S(2)}, u32[]{:S(2)}) collective-permute-start(f32[33,256]{1,0:T(8,128)S(1)} %select_add_fusion.3), channel_id=1, source_target_pairs={{0,64},{32,96},{64,0},{96,32},{128,192},{160,224},{192,128},{224,1... | collective-permute-start | bytes 101384 | tf_op jit(solution)/shard_map/ppermute | solution.py:148
  527.7 6.6 %collective-permute-start.10 = (f32[66,256]{1,0:T(8,128)S(1)}, f32[66,256]{1,0:T(8,128)S(1)}, u32[]{:S(2)}, u32[]{:S(2)}) collective-permute-start(f32[66,256]{1,0:T(8,128)S(1)} %maximum_select_fusion.3), channel_id=1, source_target_pairs={{0,256},{32,288},{64,320},{96,352},{128,384},{160,416},{192,448},{... | collective-permute-start | bytes 202760 | tf_op jit(solution)/shard_map/ppermute | solution.py:148
  534.3 6.1 %collective-permute-start.11 = (f32[132,256]{1,0:T(8,128)S(1)}, f32[132,256]{1,0:T(8,128)S(1)}, u32[]{:S(2)}, u32[]{:S(2)}) collective-permute-start(f32[132,256]{1,0:T(8,128)S(1)} %maximum_select_fusion.2), channel_id=1, source_target_pairs={{0,128},{32,160},{64,192},{96,224},{128,0},{160,32},{192,64},{224,... | collective-permute-start | bytes 405512 | tf_op jit(solution)/shard_map/ppermute | solution.py:148
  540.4 10.5 %collective-permute-start.12 = (f32[264,256]{1,0:T(8,128)S(1)}, f32[264,256]{1,0:T(8,128)S(1)}, u32[]{:S(2)}, u32[]{:S(2)}) collective-permute-start(f32[264,256]{1,0:T(8,128)S(1)} %maximum_select_fusion.1), channel_id=1, source_target_pairs={{0,32},{32,0},{64,96},{96,64},{128,160},{160,128},{192,224},{224,1... | collective-permute-start | bytes 811016 | tf_op jit(solution)/shard_map/ppermute | solution.py:148
Sparse Core Ops, SparseCore 0:
  10.1 200.2 all-gather.1
where the time goes:
time: 566 us; the launch traced here: 560 us
  waiting for transfers between devices  307 us (54%)
  starting transfers between devices  81.8 us (14%)
  other arithmetic  63.1 us (11%)
  local copies, waits for them, and re-layouts  49.9 us (9%)
  matrix products  43.1 us (8%)
  between operations  15.3 us (3%)
    all_gather x1, waiting for transfers between devices, body(): shard_piece = lax.all_gather(out_weight, 'ctx', axis=1, tiled=True)  139 us
    ppermute x5, waiting for transfers between devices, doubling_gather(): lax.ppermute(held, axis, axis_pairs(size, mask))  118 us
    unnamed x6, other arithmetic  51.7 us
    unnamed x65, local copies, waits for them, and re-layouts  37.9 us
    dot_general x24, matrix products, single(): return jnp.einsum('ckm,mj->ckj', data, table, precision=HIGHEST)  21.6 us
    ppermute x4, starting transfers between devices, summed_over_dp(): other = lax.ppermute(held, 'dp', axis_pairs(size, mask))  16.2 us
    ppermute x4, waiting for transfers between devices, summed_over_dp(): held = keep + lax.ppermute(send, 'dp', axis_pairs(size, mask))  13.5 us
    ppermute x5, starting transfers between devices, doubling_gather(): lax.ppermute(held, axis, axis_pairs(size, mask))  12.8 us
  transfers between devices with their start and end apart: 19, of which 17 were waited for; matrix products, arithmetic and copies ran while one was open for 18% of the time, Pallas kernels for 0%

commit v1 on v0

--- a/solution.py
+++ b/solution.py
@@ -160,7 +160,9 @@
     block_width = out_weight.shape[1]
     tok_rows = grad_out.shape[1]
     grad_cols = lax.all_to_all(grad_out, "ctx", split_axis=2, concat_axis=1, tiled=True)
-    shard_piece = lax.all_gather(out_weight, "ctx", axis=1, tiled=True)
+    shard_piece = jnp.concatenate(
+        lax.all_to_all(jnp.stack([out_weight] * lax.axis_size("ctx")), "ctx", 0, 0), axis=1
+    )
     blocks = shard_piece.shape[1] // block_width
     partial_value = grad_out[0]
     partial_value = partial_value.reshape(tok_rows, blocks, block_width)

time: 566 us -> 674 us (1.19)
  the two profiles are of different devices: /device:TPU:107 before, /device:TPU:63 now
where the time goes in v1:
time: 674 us; the launch traced here: 669 us
  waiting for transfers between devices  353 us (52%)
  starting transfers between devices  136 us (20%)
  other arithmetic  64.6 us (10%)
  local copies, waits for them, and re-layouts  54.1 us (8%)
  matrix products  46.1 us (7%)
  blocking collectives  12.6 us (2%)
    all_to_all x1, waiting for transfers between devices, body(): lax.all_to_all(jnp.stack([out_weight] * lax.axis_size('ctx')), 'ctx', 0, 0)  197 us
    ppermute x5, waiting for transfers between devices, doubling_gather(): lax.ppermute(held, axis, axis_pairs(size, mask))  117 us
    all_to_all x1, starting transfers between devices, body(): lax.all_to_all(grad_gated, 'ctx', split_axis=2, concat_axis=1, tiled=True)  63.2 us
    unnamed x6, other arithmetic  53.2 us
    unnamed x62, local copies, waits for them, and re-layouts  36.3 us
    dot_general x24, matrix products, single(): return jnp.einsum('ckm,mj->ckj', data, table, precision=HIGHEST)  24.2 us
    ppermute x4, starting transfers between devices, summed_over_dp(): other = lax.ppermute(held, 'dp', axis_pairs(size, mask))  16 us
  transfers between devices with their start and end apart: 18, of which 16 were waited for; matrix products, arithmetic and copies ran while one was open for 14% of the time, Pallas kernels for 0%

profile of v1, /device:TPU:63, one launch (start us, length us, event | category | flops | bytes accessed | tf_op | source)
XLA Modules:
  0.0 668.8 jit_solution(4322629779818814089)
XLA Ops:
  4.3 13.2 %all-to-all-start.4 = ((bf16[32,2,1024]{2,1,0:T(2,128)(2,1)}), bf16[32,2,1024]{2,1,0:T(2,128)(2,1)S(1)}, u32[]{:S(2)}, u32[]{:S(2)}) async-start(bf16[32,2,1024]{2,1,0:T(2,128)(2,1)} %reshape.258), calls=%async_computation.4 | async-start | bytes 262144 | tf_op jit(solution)/shard_map/all_to_all | solution.py:176
  20.7 4.7 all-to-all-done.4
  25.4 5.8 all-to-all-start.2
  33.7 5.4 all-to-all-done.2
  39.1 12.6 %all_to_all.56 = bf16[32,2,1024]{2,1,0:T(2,128)(2,1)S(1)} all-to-all(bf16[32,2,1024]{2,1,0:T(2,128)(2,1)S(1)} %reshape.254), channel_id=1, replica_groups=mesh['dp'=16,'ctx'=32] {'ctx'}, dimensions={0} | all-to-all | bytes 262144 | tf_op jit(solution)/shard_map/all_to_all | solution.py:178
  51.8 5.1 stack.2
  56.9 7.6 %all-to-all-start = ((bf16[32,512,256]{2,1,0:T(8,128)(2,1)}), bf16[32,512,256]{2,1,0:T(8,128)(2,1)}, u32[]{:S(2)}, u32[]{:S(2)}) async-start(bf16[32,512,256]{2,1,0:T(8,128)(2,1)} %stack.2), calls=%async_computation | async-start | bytes 16777216 | tf_op jit(solution)/shard_map/all_to_all | solution.py:164
  64.5 1.9 copy.78
  73.9 197.1 %all-to-all-done = bf16[32,512,256]{2,1,0:T(8,128)(2,1)} async-done(((bf16[32,512,256]{2,1,0:T(8,128)(2,1)}), bf16[32,512,256]{2,1,0:T(8,128)(2,1)}, u32[]{:S(2)}, u32[]{:S(2)}) %all-to-all-start) | async-done | bytes 8388640 | tf_op jit(solution)/shard_map/all_to_all | solution.py:164
  270.9 9.3 %fusion.2 = bf16[32,128,512]{2,1,0:T(8,128)(2,1)} fusion(bf16[32,512,256]{2,1,0:T(8,128)(2,1)} %all-to-all-done, bf16[128,32,256]{2,1,0:T(8,128)(2,1)} %bitcast.292), kind=kOutput, calls=%fused_computation.7 | convolution fusion | flops 1075838976 | bytes 14680064 | tf_op jit(solution)/shard_map/tks,cks->ktc/dot_general | solution.py:170
  280.2 3.5 reduce_sum.39
  285.5 3.0 reduce.12
  290.0 63.2 %all-to-all-start.1 = ((bf16[32,2,1024]{2,1,0:T(2,128)(2,1)}), bf16[32,2,1024]{2,1,0:T(2,128)(2,1)}, u32[]{:S(2)}, u32[]{:S(2)}) async-start(bf16[32,2,1024]{2,1,0:T(2,128)(2,1)} %reshape.260), calls=%async_computation.1 | async-start | bytes 262144 | tf_op jit(solution)/shard_map/all_to_all | solution.py:179
  353.2 2.7 convolution_subtract_fusion.5
  355.9 5.2 all-to-all-done.1
  373.9 2.6 multiply_reduce_fusion.1
  388.5 2.1 collective-permute-start
  390.7 7.5 %collective-permute-done = bf16[16,4096]{1,0:T(8,128)(2,1)S(1)} collective-permute-done((bf16[16,4096]{1,0:T(8,128)(2,1)S(1)}, bf16[16,4096]{1,0:T(8,128)(2,1)S(1)}, u32[]{:S(2)}, u32[]{:S(2)}) %collective-permute-start) | collective-permute-done | bytes 131104 | tf_op jit(solution)/shard_map/ppermute | solution.py:108
  398.3 1.9 collective-permute-start.1
  400.2 12.3 %collective-permute-done.1 = bf16[32,4096]{1,0:T(8,128)(2,1)S(1)} collective-permute-done((bf16[32,4096]{1,0:T(8,128)(2,1)S(1)}, bf16[32,4096]{1,0:T(8,128)(2,1)S(1)}, u32[]{:S(2)}, u32[]{:S(2)}) %collective-permute-start.1) | collective-permute-done | bytes 262176 | tf_op jit(solution)/shard_map/ppermute | solution.py:108
  413.4 3.3 collective-permute-start.2
  416.7 7.0 %copy.75 = bf16[1,128,8192]{1,0,2:T(2,128)(2,1)} copy(bf16[1,128,8192]{2,1,0:T(8,128)(2,1)S(1)} %copy-done) | data formatting | bytes 4194304 | tf_op args[3]
  423.7 45.2 %reduce.13 = bf16[8192,128]{1,0:T(8,128)(2,1)S(1)} reduce(bf16[8192,1,128]{2,1,0:T(2,128)(2,1)} %bitcast.289, bf16[]{:T(256)} %broadcast.473), dimensions={1}, to_apply=%bitcast.258.reduce_sub_computation | reduce | bytes 4194306
  468.9 2.1 reshape.262
  471.0 6.1 all-to-all-start.5
  478.2 3.1 collective-permute-start.3
  482.7 1.9 constant_dynamic-update-slice_fusion.1
  484.7 63.5 %collective-permute-done.3 = bf16[128,4096]{1,0:T(8,128)(2,1)S(1)} collective-permute-done((bf16[128,4096]{1,0:T(8,128)(2,1)S(1)}, bf16[128,4096]{1,0:T(8,128)(2,1)S(1)}, u32[]{:S(2)}, u32[]{:S(2)}) %collective-permute-start.3) | collective-permute-done | bytes 1048608 | tf_op jit(solution)/shard_map/ppermute | solution.py:108
  549.4 2.0 copy-done.15
  553.5 6.8 %reshape.263 = bf16[8192,1,128]{2,1,0:T(2,128)(2,1)} reshape(bf16[32,2,16384]{2,1,0:T(2,128)(2,1)S(1)} %all-to-all-done.5) | data formatting | bytes 4194304
  560.4 2.5 copy.77
  562.8 2.9 copy.76
  566.0 33.2 %collective-permute-done.4 = bf16[256,4096]{1,0:T(8,128)(2,1)} collective-permute-done((bf16[256,4096]{1,0:T(8,128)(2,1)}, bf16[256,4096]{1,0:T(8,128)(2,1)}, u32[]{:S(2)}, u32[]{:S(2)}) %collective-permute-start.4) | collective-permute-done | bytes 2097184 | tf_op jit(solution)/shard_map/ppermute | solution.py:108
  599.2 3.1 constant_dynamic-update-slice_fusion.5
  602.3 3.4 fusion.328
  606.6 4.3 collective-permute-start.5
  612.2 2.4 collective-permute-start.6
  615.4 3.6 collective-permute-done.6
  619.0 3.2 collective-permute-start.7
  623.0 2.7 collective-permute-done.7
  625.8 2.3 collective-permute-start.8
  628.9 5.7 collective-permute-done.8
  637.3 6.5 collective-permute-done.9
  643.8 3.1 collective-permute-start.10
  648.0 2.4 collective-permute-done.10
  650.4 2.1 collective-permute-start.11
  653.6 2.6 collective-permute-done.11
  656.3 8.9 %collective-permute-start.12 = (f32[264,256]{1,0:T(8,128)S(1)}, f32[264,256]{1,0:T(8,128)S(1)}, u32[]{:S(2)}, u32[]{:S(2)}) collective-permute-start(f32[264,256]{1,0:T(8,128)S(1)} %maximum_select_fusion.1), channel_id=1, source_target_pairs={{0,32},{32,0},{64,96},{96,64},{128,160},{160,128},{192,224},{224,1... | collective-permute-start | bytes 811016 | tf_op jit(solution)/shard_map/ppermute | solution.py:148
  (154 shorter events, 64.3 us)
Async XLA Ops:
  4.3 21.0 %all-to-all-start.4 = ((bf16[32,2,1024]{2,1,0:T(2,128)(2,1)}), bf16[32,2,1024]{2,1,0:T(2,128)(2,1)S(1)}, u32[]{:S(2)}, u32[]{:S(2)}) async-start(bf16[32,2,1024]{2,1,0:T(2,128)(2,1)} %reshape.258), calls=%async_computation.4 | async-start | bytes 262144 | tf_op jit(solution)/shard_map/all_to_all | solution.py:176
  25.4 13.8 %all-to-all-start.2 = ((bf16[32,2,1024]{2,1,0:T(2,128)(2,1)}), bf16[32,2,1024]{2,1,0:T(2,128)(2,1)S(1)}, u32[]{:S(2)}, u32[]{:S(2)}) async-start(bf16[32,2,1024]{2,1,0:T(2,128)(2,1)} %reshape.256), calls=%async_computation.2 | async-start | bytes 262144 | tf_op jit(solution)/shard_map/all_to_all | solution.py:177
  56.9 7.7 %copy-start = (bf16[1,128,8192]{2,1,0:T(8,128)(2,1)S(1)}, bf16[1,128,8192]{2,1,0:T(8,128)(2,1)}, u32[]{:S(2)}) copy-start(bf16[1,128,8192]{2,1,0:T(8,128)(2,1)} %param.10) | copy-start | bytes 6291460
  56.9 214.0 %all-to-all-start = ((bf16[32,512,256]{2,1,0:T(8,128)(2,1)}), bf16[32,512,256]{2,1,0:T(8,128)(2,1)}, u32[]{:S(2)}, u32[]{:S(2)}) async-start(bf16[32,512,256]{2,1,0:T(8,128)(2,1)} %stack.2), calls=%async_computation | async-start | bytes 16777216 | tf_op jit(solution)/shard_map/all_to_all | solution.py:164
  64.5 2.0 copy-start.14
  67.3 0.7 copy-start.6
  67.6 0.7 copy-start.8
  290.0 71.1 %all-to-all-start.1 = ((bf16[32,2,1024]{2,1,0:T(2,128)(2,1)}), bf16[32,2,1024]{2,1,0:T(2,128)(2,1)}, u32[]{:S(2)}, u32[]{:S(2)}) async-start(bf16[32,2,1024]{2,1,0:T(2,128)(2,1)} %reshape.260), calls=%async_computation.1 | async-start | bytes 262144 | tf_op jit(solution)/shard_map/all_to_all | solution.py:179
  362.8 0.7 copy-start.4
  363.6 4.1 copy-start.2
  363.6 4.1 copy-start.3
  370.3 3.6 copy-start.13
  387.7 10.6 %copy-start.10 = (f32[2,8,64,128]{3,1,2,0:T(8,128)}, f32[2,8,64,128]{3,1,2,0:T(8,128)S(1)}, u32[]{:S(2)}) copy-start(f32[2,8,64,128]{3,1,2,0:T(8,128)S(1)} %copy.111) | copy-start | bytes 1572868
  388.5 9.7 %collective-permute-start = (bf16[16,4096]{1,0:T(8,128)(2,1)S(1)}, bf16[16,4096]{1,0:T(8,128)(2,1)S(1)}, u32[]{:S(2)}, u32[]{:S(2)}) collective-permute-start(bf16[16,4096]{1,0:T(8,128)(2,1)S(1)} %get-tuple-element.12), channel_id=1, source_target_pairs={{0,16},{1,17},{2,18},{3,19},{4,20},{5,21},{6,22},{7,23},{8,24},{9,... | collective-permute-start | bytes 393224 | tf_op jit(solution)/shard_map/ppermute | solution.py:108
  398.3 14.3 %collective-permute-start.1 = (bf16[32,4096]{1,0:T(8,128)(2,1)S(1)}, bf16[32,4096]{1,0:T(8,128)(2,1)S(1)}, u32[]{:S(2)}, u32[]{:S(2)}) collective-permute-start(bf16[32,4096]{1,0:T(8,128)(2,1)S(1)} %pad_maximum_fusion.4), channel_id=1, source_target_pairs={{0,8},{1,9},{2,10},{3,11},{4,12},{5,13},{6,14},{7,15},{8,0},{9,1},... | collective-permute-start | bytes 786440 | tf_op jit(solution)/shard_map/ppermute | solution.py:108
  413.4 63.7 %collective-permute-start.2 = (bf16[64,4096]{1,0:T(8,128)(2,1)}, bf16[64,4096]{1,0:T(8,128)(2,1)}, u32[]{:S(2)}, u32[]{:S(2)}) collective-permute-start(bf16[64,4096]{1,0:T(8,128)(2,1)} %pad_maximum_fusion.1), channel_id=1, source_target_pairs={{0,2},{1,3},{2,0},{3,1},{4,6},{5,7},{6,4},{7,5},{8,10},{9,11},{10,... | collective-permute-start | bytes 1572872 | tf_op jit(solution)/shard_map/ppermute | solution.py:108
  471.0 82.6 %all-to-all-start.5 = ((bf16[32,2,16384]{2,1,0:T(2,128)(2,1)}), bf16[32,2,16384]{2,1,0:T(2,128)(2,1)S(1)}, u32[]{:S(2)}, u32[]{:S(2)}) async-start(bf16[32,2,16384]{2,1,0:T(2,128)(2,1)} %reshape.262), calls=%async_computation.5 | async-start | bytes 4194304 | tf_op jit(solution)/shard_map/all_to_all | solution.py:162
  478.2 70.0 %collective-permute-start.3 = (bf16[128,4096]{1,0:T(8,128)(2,1)S(1)}, bf16[128,4096]{1,0:T(8,128)(2,1)S(1)}, u32[]{:S(2)}, u32[]{:S(2)}) collective-permute-start(bf16[128,4096]{1,0:T(8,128)(2,1)S(1)} %pad_maximum_fusion), channel_id=1, source_target_pairs={{0,4},{1,5},{2,6},{3,7},{4,0},{5,1},{6,2},{7,3},{8,12},{9,13},{10,... | collective-permute-start | bytes 3145736 | tf_op jit(solution)/shard_map/ppermute | solution.py:108
  549.4 2.0 copy-start.15
  551.3 47.9 %collective-permute-start.4 = (bf16[256,4096]{1,0:T(8,128)(2,1)}, bf16[256,4096]{1,0:T(8,128)(2,1)}, u32[]{:S(2)}, u32[]{:S(2)}) collective-permute-start(bf16[256,4096]{1,0:T(8,128)(2,1)} %get-tuple-element.19), channel_id=1, source_target_pairs={{0,1},{1,0},{2,3},{3,2},{4,5},{5,4},{6,7},{7,6},{8,9},{9,8},{10,11... | collective-permute-start | bytes 6291464 | tf_op jit(solution)/shard_map/ppermute | solution.py:108
  565.8 36.5 %copy-start.12 = (bf16[1,32,128,256]{3,2,1,0:T(8,128)(2,1)S(1)}, bf16[1,32,128,256]{3,2,1,0:T(8,128)(2,1)}, u32[]{:S(2)}) copy-start(bf16[1,32,128,256]{3,2,1,0:T(8,128)(2,1)} %copy.76) | copy-start | bytes 6291460
  605.8 8.8 %copy-start.1 = (f32[16,64,128]{2,1,0:T(8,128)S(1)}, f32[16,64,128]{2,1,0:T(8,128)}, u32[]{:S(2)}) copy-start(f32[16,64,128]{2,1,0:T(8,128)} %get-tuple-element.14) | copy-start | bytes 1572868
  606.6 5.4 collective-permute-start.5
  612.2 6.8 %collective-permute-start.6 = (f32[132,256]{1,0:T(8,128)S(1)}, f32[132,256]{1,0:T(8,128)S(1)}, u32[]{:S(2)}, u32[]{:S(2)}) collective-permute-start(f32[132,256]{1,0:T(8,128)S(1)} %slice_select_fusion.1), channel_id=1, source_target_pairs={{0,128},{32,160},{64,192},{96,224},{128,0},{160,32},{192,64},{224,... | collective-permute-start | bytes 405512 | tf_op jit(solution)/shard_map/ppermute | solution.py:146
  619.0 33.6 %copy-start.7 = (f32[1,32,128,16]{2,1,3,0:T(8,128)S(1)}, f32[1,32,128,16]{2,1,3,0:T(8,128)}, u32[]{:S(2)}) copy-start(f32[1,32,128,16]{2,1,3,0:T(8,128)} %copy-done.6) | copy-start | bytes 786436
  619.0 33.6 %copy-start.9 = (f32[1,32,128,16]{2,1,3,0:T(8,128)S(1)}, f32[1,32,128,16]{2,1,3,0:T(8,128)}, u32[]{:S(2)}) copy-start(f32[1,32,128,16]{2,1,3,0:T(8,128)} %copy-done.8) | copy-start | bytes 786436
  619.0 6.7 %collective-permute-start.7 = (f32[66,256]{1,0:T(8,128)S(1)}, f32[66,256]{1,0:T(8,128)S(1)}, u32[]{:S(2)}, u32[]{:S(2)}) collective-permute-start(f32[66,256]{1,0:T(8,128)S(1)} %slice_select_fusion.2), channel_id=1, source_target_pairs={{0,256},{32,288},{64,320},{96,352},{128,384},{160,416},{192,448},{... | collective-permute-start | bytes 202760 | tf_op jit(solution)/shard_map/ppermute | solution.py:146
  625.8 39.4 %copy-start.5 = (f32[1,32,128,16]{2,1,3,0:T(8,128)S(1)}, f32[1,32,128,16]{2,1,3,0:T(8,128)}, u32[]{:S(2)}) copy-start(f32[1,32,128,16]{2,1,3,0:T(8,128)} %copy-done.4) | copy-start | bytes 786436
  625.8 39.4 %copy-start.11 = (f32[2,8,64,128]{3,1,2,0:T(8,128)S(1)}, f32[2,8,64,128]{3,1,2,0:T(8,128)}, u32[]{:S(2)}) copy-start(f32[2,8,64,128]{3,1,2,0:T(8,128)} %copy-done.10) | copy-start | bytes 1572868
  625.8 8.8 %collective-permute-start.8 = (f32[33,256]{1,0:T(8,128)S(1)}, f32[33,256]{1,0:T(8,128)S(1)}, u32[]{:S(2)}, u32[]{:S(2)}) collective-permute-start(f32[33,256]{1,0:T(8,128)S(1)} %slice_select_fusion.3), channel_id=1, source_target_pairs={{0,64},{32,96},{64,0},{96,32},{128,192},{160,224},{192,128},{224,1... | collective-permute-start | bytes 101384 | tf_op jit(solution)/shard_map/ppermute | solution.py:146
  634.6 9.2 %collective-permute-start.9 = (f32[33,256]{1,0:T(8,128)S(1)}, f32[33,256]{1,0:T(8,128)S(1)}, u32[]{:S(2)}, u32[]{:S(2)}) collective-permute-start(f32[33,256]{1,0:T(8,128)S(1)} %select_add_fusion.3), channel_id=1, source_target_pairs={{0,64},{32,96},{64,0},{96,32},{128,192},{160,224},{192,128},{224,1... | collective-permute-start | bytes 101384 | tf_op jit(solution)/shard_map/ppermute | solution.py:148
  643.8 6.6 collective-permute-start.10
  650.4 5.8 collective-permute-start.11
  656.3 10.1 %collective-permute-start.12 = (f32[264,256]{1,0:T(8,128)S(1)}, f32[264,256]{1,0:T(8,128)S(1)}, u32[]{:S(2)}, u32[]{:S(2)}) collective-permute-start(f32[264,256]{1,0:T(8,128)S(1)} %maximum_select_fusion.1), channel_id=1, source_target_pairs={{0,32},{32,0},{64,96},{96,64},{128,160},{160,128},{192,224},{224,1... | collective-permute-start | bytes 811016 | tf_op jit(solution)/shard_map/ppermute | solution.py:148
